TPU v7x, 512 devices: a whole 4x4x16 slice. The times are simulated.
512 devices in a mesh: cfg: 2 (over core), grp: 4 (over y), seq: 64 (over x, z).
Axes of the slice: x: 4, y: 4, z: 16, core: 2. Of those that a mesh axis runs over, the one named last changes fastest.
Arguments:
- query: bfloat16 [2, 4, 2, 128, 2432], P('cfg', 'grp', None, 'seq'), may hold values from -150 to 150
- keys: bfloat16 [2, 4, 2, 128, 2432], P('cfg', 'grp', None, 'seq'), may hold values from -5.5 to 5.5
- values: bfloat16 [2, 4, 2, 128, 2432], P('cfg', 'grp', None, 'seq'), may hold values from -5 to 5
- hidden: bfloat16 [2, 4, 2, 128, 2432], P('cfg', 'grp', None, 'seq'), may hold values from -23 to 23
- latent: float32 [4, 2, 128, 64], P('grp', None, 'seq', 'cfg'), may hold values from -6 to 6
- deal: int32 [4, 2], replicated, may hold values from 0 to 5, as said below
- lengths: int32 [4, 2], replicated, may hold values from 64 to 128, as said below
- w_out: bfloat16 [2432, 2432], P(('cfg', 'seq')), may hold values from -0.125 to 0.125
- attn_gate: float32 [2, 6, 2432], P('cfg'), may hold values from 0.25 to 1.75
- modulation: float32 [2, 6, 2, 2432], P('cfg'), may hold values from -3 to 3
- w_final: bfloat16 [2432, 64], replicated, may hold values from -0.125 to 0.125
- guide: float32 [6], replicated, may hold values from 2 to 7
- step_size: float32 [6], replicated, may hold values from 0.15 to 0.5
Outputs:
- latent_next: float32 [4, 2, 128, 64], P('grp', None, 'seq', 'cfg')
Inputs may be any that keep to these rules, and one draw needn't show every extreme that they name: `deal`: column 0 of row g names the whole item of group g, column 1 the item split between groups g and g xor 1 (equal in both rows); every one of the 6 items is named by exactly one column-0 entry or one pair of column-1 entries. `lengths`: in each column some group has all 128 slots live.
All inputs are finite; a program needn't handle non-finite values.
Results may differ from a plain program's by a relative error of at most 0.0049.
Values may be sent and summed in bfloat16 or wider, within the bound.
No kernel may reach another device: no remote copies, remote signals or barrier semaphores. Data moves between devices by JAX's collectives and lax.ppermute only.
A program may use at most 128 MiB of HBM per device.

v0:
```python
import jax
import jax.numpy as jnp
from jax import lax
from jax.sharding import PartitionSpec as P

D = 2432
HEADS = 38
HD = 64
NORM_EPS = 1e-06


def from_partner(x, axis, apart):
    return lax.ppermute(x, axis, [(i, i ^ 1 << apart) for i in range(lax.axis_size(axis))])


def attend(queries, keys_all, values_all, live_keys):
    row_count = queries.shape[0]
    query_heads = queries.reshape(row_count, HEADS, HD)
    key_heads = keys_all.reshape(-1, HEADS, HD)
    value_heads = values_all.reshape(-1, HEADS, HD)
    scores = jnp.einsum(
        "shd,khd->hsk", query_heads, key_heads, preferred_element_type=jnp.float32
    ) * HD ** (-0.5)
    scores = jnp.where(live_keys[None, None, :], scores, -jnp.inf)
    peak_score = jnp.max(scores, axis=2, keepdims=True)
    raw_weights = jnp.exp(scores - peak_score)
    row_total = jnp.sum(raw_weights, axis=2, keepdims=True)
    weights = raw_weights.astype(jnp.bfloat16)
    mixed_out = (
        jnp.einsum("hsk,khd->hsd", weights, value_heads, preferred_element_type=jnp.float32)
        / row_total
    )
    return jnp.transpose(mixed_out, (1, 0, 2)).reshape(row_count, HEADS * HD)


def shards(
    query,
    keys,
    values,
    hidden,
    latent,
    deal,
    lengths,
    w_out,
    attn_gate,
    modulation,
    w_final,
    guide,
    step_size,
):
    group_id = lax.axis_index("grp")
    branch = lax.axis_index("cfg")
    partner = jnp.bitwise_xor(group_id, 1)
    own_lengths = lax.dynamic_index_in_dim(lengths, group_id, 0, keepdims=False)
    pair_lengths = lax.dynamic_index_in_dim(lengths, partner, 0, keepdims=False)
    item_ids = lax.dynamic_index_in_dim(deal, group_id, 0, keepdims=False)
    resident_key_rows = keys[0, 0]
    local_values = values[0, 0]
    shard_rows = resident_key_rows.shape[1]
    far_keys, far_values = from_partner((resident_key_rows[1], local_values[1]), "grp", 0)
    combined_key_rows, joint_values = (
        lax.all_gather(
            jnp.concatenate([resident_key_rows, far_keys[None]], 0), "seq", axis=1, tiled=True
        ),
        lax.all_gather(
            jnp.concatenate([local_values, far_values[None]], 0), "seq", axis=1, tiled=True
        ),
    )
    group_keys, group_values = (combined_key_rows[:2], joint_values[:2])
    pair_keys, pair_values = (combined_key_rows[2], joint_values[2])
    slot_total = group_keys.shape[1]
    slot_ids = jnp.arange(slot_total)
    live_home = slot_ids < own_lengths[0]
    live_own = slot_ids < own_lengths[1]
    live_pair = slot_ids < pair_lengths[1]
    local_query = query[0, 0]
    local_output_rows = attend(local_query[0], group_keys[0], group_values[0], live_home)
    shared = attend(
        local_query[1],
        jnp.concatenate([group_keys[1], pair_keys], 0),
        jnp.concatenate([group_values[1], pair_values], 0),
        jnp.concatenate([live_own, live_pair], 0),
    )
    attn_rows = (
        jnp.stack([local_output_rows, shared]).astype(jnp.bfloat16).reshape(2 * shard_rows, D)
    )
    projected = jnp.dot(
        attn_rows,
        lax.all_gather(w_out, ("cfg", "seq"), axis=0, tiled=True),
        preferred_element_type=jnp.float32,
    )
    projected = projected.reshape(2, shard_rows, D)
    item_count = guide.shape[0]
    indicator_mask = (jnp.arange(item_count)[None, :] == item_ids[:, None]).astype(jnp.float32)
    gate_now = jnp.einsum(
        "ri,id->rd", indicator_mask, attn_gate[0], precision=lax.Precision.HIGHEST
    )
    stream = hidden[0, 0].astype(jnp.float32) + gate_now[:, None, :] * projected
    row_mean = jnp.mean(stream, axis=2, keepdims=True)
    centred = stream - row_mean
    row_var = jnp.mean(centred * centred, axis=2, keepdims=True)
    normed = centred * lax.rsqrt(row_var + NORM_EPS)
    selected_entries = jnp.einsum(
        "ub,bkg->ukg", indicator_mask, modulation[0], precision=lax.Precision.HIGHEST
    )
    shaped = (
        normed * (1.0 + selected_entries[:, 1][:, None, :]) + selected_entries[:, 0][:, None, :]
    ).astype(jnp.bfloat16)
    velocity = jnp.einsum("rsd,dc->rsc", shaped, w_final, preferred_element_type=jnp.float32)
    row_slots = lax.axis_index("seq") * shard_rows + jnp.arange(shard_rows)
    live_rows = jnp.stack([row_slots < own_lengths[0], row_slots < own_lengths[1]])
    velocity = jnp.where(live_rows[:, :, None], velocity, jnp.float32(0.0))
    weight_now = jnp.sum(indicator_mask * guide[None, :], axis=1)[:, None, None]
    step_now = jnp.sum(indicator_mask * step_size[None, :], axis=1)[:, None, None]
    latent_part = latent[0]
    part_width = latent_part.shape[2]
    outgoing_velocity = lax.dynamic_slice_in_dim(velocity, (1 - branch) * part_width, part_width, 2)
    own_velocity = lax.dynamic_slice_in_dim(velocity, branch * part_width, part_width, 2)
    other_velocity = from_partner(outgoing_velocity, "cfg", 0)
    is_conditional = branch == 0
    cond_velocity = jnp.where(is_conditional, own_velocity, other_velocity)
    uncond_velocity = jnp.where(is_conditional, other_velocity, own_velocity)
    guided = uncond_velocity + weight_now * (cond_velocity - uncond_velocity)
    updated = latent_part - step_now * guided
    return updated[None]


def solution(mesh):
    placed = (
        P("cfg", "grp", None, "seq", None),
        P("cfg", "grp", None, "seq", None),
        P("cfg", "grp", None, "seq", None),
        P("cfg", "grp", None, "seq", None),
        P("grp", None, "seq", "cfg"),
        P(),
        P(),
        P(("cfg", "seq"), None),
        P("cfg", None, None),
        P("cfg", None, None, None),
        P(),
        P(),
        P(),
    )
    return jax.shard_map(
        shards, mesh=mesh, in_specs=placed, out_specs=P("grp", None, "seq", "cfg"), check_vma=False
    )
```

profile of v0, /device:TPU:1, one launch (start us, length us, event | category | flops | bytes accessed | tf_op | source)
XLA Modules:
  0.0 488.3 jit_solution(13304708734672202299)
XLA Ops:
  6.5 0.8 slice_bitcast_fusion.1
  7.3 4.0 collective-permute-start.1
  13.8 3.4 collective-permute-start
  20.5 0.8 constant_dynamic-slice_fusion.2
  21.9 0.9 fusion.57
  24.1 1.3 iota_compare_fusion.3
  25.4 1.3 fusion.58
  26.8 1.0 fusion.34
  27.8 1.2 fusion.32
  29.0 122.6 %all-gather.7.cloned.1.call-done = bf16[3,128,2432]{2,0,1:T(4,128)(2,1)} async-done(((bf16[3,2,2432]{2,0,1:T(4,128)(2,1)}), bf16[3,128,2432]{2,0,1:T(4,128)(2,1)}) %all-gather.7.cloned.1.call-update) | async-done | bytes 1867792 | tf_op jit(solution)/shard_map/all_gather | solution.py:65
  151.6 7.6 %fusion.66 = (bf16[1,128,2432]{2,0,1:T(2,128)(2,1)S(1)}, bf16[1,128,2432]{2,0,1:T(2,128)(2,1)}, bf16[1,128,2432]{2,0,1:T(2,128)(2,1)S(1)}) fusion(bf16[3,128,2432]{2,0,1:T(4,128)(2,1)} %all-gather.7.cloned.1.call-done), kind=kLoop, calls=%fused_computation.84 | loop fusion | bytes 3735552 | tf_op jit(solution)/shard_map/slice | solution.py:77
  159.2 2.7 copy.57
  162.0 2.1 copy.56
  164.0 127.7 %all-gather.5.cloned.1.call-done = bf16[3,128,2432]{2,0,1:T(4,128)(2,1)} async-done(((bf16[3,2,2432]{2,0,1:T(4,128)(2,1)}), bf16[3,128,2432]{2,0,1:T(4,128)(2,1)}) %all-gather.5.cloned.1.call-update) | async-done | bytes 1867792 | tf_op jit(solution)/shard_map/all_gather | solution.py:62
  291.8 8.0 %fusion.65 = (bf16[1,128,2432]{2,0,1:T(2,128)(2,1)S(1)}, bf16[1,128,2432]{2,0,1:T(2,128)(2,1)}, bf16[1,128,2432]{2,0,1:T(2,128)(2,1)}) fusion(bf16[3,128,2432]{2,0,1:T(4,128)(2,1)} %all-gather.5.cloned.1.call-done), kind=kLoop, calls=%fused_computation.83 | loop fusion | bytes 3735552 | tf_op jit(solution)/shard_map/slice | solution.py:77
  299.8 3.6 copy.54
  303.4 3.6 copy.53
  306.9 1.7 fusion.69
  309.4 1.4 copy.51
  310.9 1.4 copy.47
  313.4 141.1 %all-gather.9.cloned.1.call-done = bf16[128,19,2432]{2,1,0:T(8,128)(2,1)} async-done(((bf16[1,19,2432]{2,1,0:T(8,128)(2,1)}), bf16[128,19,2432]{2,1,0:T(8,128)(2,1)}) %all-gather.9.cloned.1.call-update) | async-done | bytes 11829264 | tf_op jit(solution)/shard_map/all_gather | solution.py:89
  454.5 16.7 %reshape.76 = bf16[2432,2432,1]{1,0,2:T(8,128)(2,1)} reshape(bf16[128,19,2432]{2,1,0:T(8,128)(2,1)} %all-gather.9.cloned.1.call-done) | data formatting | bytes 23658496
  471.3 6.2 %fusion.71 = (f32[2,2]{1,0:T(2,128)S(1)}, f32[2,2,2432]{2,1,0:T(2,128)S(1)}) fusion(bf16[2432,2432,1]{1,0,2:T(8,128)(2,1)} %reshape.76, bf16[1,2,2432]{2,1,0:T(2,128)(2,1)S(1)} %stack_reshape.9, bf16[1,2,2432]{2,1,0:T(2,128)(2,1)S(1)} %stack_reshape.8, f32[2,2432]{1,0:T(2,128)S(1)} %fusion.34, bf16[1,1,2,2,2432]{4,3,2,1,0:T(2,128)(2,1)S(1)} %copy-done.2), kind=kOutput, calls=%fused_computation.89 | convolution fusion | flops 47394812 | bytes 11926544 | tf_op jit(solution)/shard_map/dot_general | solution.py:87
  478.1 2.2 collective-permute-start.2
  (53 shorter events, 11.7 us)
Async XLA Ops:
  6.5 471.2 %copy-start = (bf16[2432,64]{0,1:T(8,128)(2,1)S(1)}, bf16[2432,64]{0,1:T(8,128)(2,1)}, u32[]{:S(2)}) copy-start(bf16[2432,64]{0,1:T(8,128)(2,1)} %param.23) | copy-start | bytes 933892
  6.5 145.1 %all-gather.7.cloned.1.call-start = ((), (), s32[]{:S(2)}) async-start(), calls=%async_computation.1 | async-start | bytes 2529280 | tf_op jit(solution)/shard_map/all_gather | solution.py:65
  7.3 5.1 %collective-permute-start.1 = (bf16[2,2432]{1,0:T(2,128)(2,1)S(1)}, bf16[2,2432]{1,0:T(2,128)(2,1)S(1)}, u32[]{:S(2)}, u32[]{:S(2)}) collective-permute-start(bf16[2,2432]{1,0:T(2,128)(2,1)S(1)} %slice_bitcast_fusion.1), channel_id=1, source_target_pairs={{0,64},{64,0},{128,192},{192,128},{1,65},{65,1},{129,193},{193,129... | collective-permute-start | bytes 29192 | tf_op jit(solution)/shard_map/ppermute | solution.py:13
  13.1 278.7 %all-gather.5.cloned.1.call-start = ((), (), s32[]{:S(2)}) async-start(), calls=%async_computation | async-start | bytes 2529280 | tf_op jit(solution)/shard_map/all_gather | solution.py:62
  13.8 4.4 collective-permute-start
  18.9 435.6 %all-gather.9.cloned.1.call-start = ((), (), s32[]{:S(2)}) async-start(), calls=%async_computation.2 | async-start | bytes 15058944 | tf_op jit(solution)/shard_map/all_gather | solution.py:89
  306.9 1.9 copy-start.1
  313.4 157.8 %copy-start.2 = (bf16[1,1,2,2,2432]{4,3,2,1,0:T(2,128)(2,1)S(1)}, bf16[1,1,2,2,2432]{4,3,2,1,0:T(2,128)(2,1)}, u32[]{:S(2)}) copy-start(bf16[1,1,2,2,2432]{4,3,2,1,0:T(2,128)(2,1)} %param.16) | copy-start | bytes 58372
  471.2 9.0 %copy-start.4 = (f32[6]{0:T(128)S(1)}, f32[6]{0:T(128)}, u32[]{:S(2)}) copy-start(f32[6]{0:T(128)} %param.25) | copy-start | bytes 76
  471.2 9.0 %copy-start.5 = (f32[6]{0:T(128)S(1)}, f32[6]{0:T(128)}, u32[]{:S(2)}) copy-start(f32[6]{0:T(128)} %param.24) | copy-start | bytes 76
  471.2 9.9 %copy-start.3 = (f32[1,2,2,32]{3,2,1,0:T(2,128)S(1)}, f32[1,2,2,32]{3,2,1,0:T(2,128)}, u32[]{:S(2)}) copy-start(f32[1,2,2,32]{3,2,1,0:T(2,128)} %param.17) | copy-start | bytes 1540
  478.1 3.1 collective-permute-start.2
Sparse Core Ops, SparseCore 0:
  13.2 138.4 all-gather.6
  154.6 137.1 all-gather.4
  294.8 159.6 all-gather.8
where the time goes:
time: 490 us; the launch traced here: 488 us
  waiting for transfers between devices  393 us (80%)
  local copies, waits for them, and re-layouts  54.1 us (11%)
  between operations  13.3 us (3%)
  matrix products  11.7 us (2%)
  starting transfers between devices  9.63 us (2%)
  other arithmetic  6.06 us (1%)
    all_gather x1, waiting for transfers between devices, shards(): lax.all_gather(w_out, ('cfg', 'seq'), axis=0, tiled=True)  141 us
    all_gather x1, waiting for transfers between devices, shards(): lax.all_gather(jnp.concatenate([resident_key_rows, far_keys[None]], 0), '...  128 us
    all_gather x1, waiting for transfers between devices, shards(): lax.all_gather(jnp.concatenate([local_values, far_values[None]], 0), 'seq...  123 us
    unnamed x15, local copies, waits for them, and re-layouts  18.2 us
  transfers between devices with their start and end apart: 6, of which 6 were waited for; matrix products, arithmetic and copies ran while one was open for 9% of the time, Pallas kernels for 0%

commit v1 on v0

--- a/solution.py
+++ b/solution.py
@@ -58,10 +58,14 @@
     local_values = values[0, 0]
     shard_rows = resident_key_rows.shape[1]
     far_keys, far_values = from_partner((resident_key_rows[1], local_values[1]), "grp", 0)
+
+    def play_the_scenes(view):
+        return jnp.concatenate(
+            lax.all_to_all(jnp.stack(lax.axis_size("seq") * [view]), "seq", 0, 0), axis=1
+        )
+
     combined_key_rows, joint_values = (
-        lax.all_gather(
-            jnp.concatenate([resident_key_rows, far_keys[None]], 0), "seq", axis=1, tiled=True
-        ),
+        play_the_scenes(jnp.concatenate([resident_key_rows, far_keys[None]], 0)),
         lax.all_gather(
             jnp.concatenate([local_values, far_values[None]], 0), "seq", axis=1, tiled=True
         ),

time: 490 us -> 362 us (0.74)
  waiting for transfers between devices: 393 us -> 252 us
  starting transfers between devices: 9.63 us -> 28 us
    all_gather x1 -> x0, waiting for transfers between devices: 128 us -> none  [shards(): lax.all_gather(jnp.concatenate([resident_key_rows, far_keys[None]], 0), '...]
    all_to_all x0 -> x1, starting transfers between devices: none -> 18.4 us  [play_the_scenes(): lax.all_to_all(jnp.stack(lax.axis_size('seq') * [view]), 'seq', 0, 0)]
    all_gather x1, waiting for transfers between devices: 141 us -> 131 us  [shards(): lax.all_gather(w_out, ('cfg', 'seq'), axis=0, tiled=True)]
    concatenate x0 -> x4, local copies, waits for them, and re-layouts: none -> 7.36 us  [shards(): jnp.concatenate([group_keys[1], pair_keys], 0)]
    slice x2 -> x1, local copies, waits for them, and re-layouts: 9.4 us -> 2.13 us  [shards(): group_keys[0]]
    unnamed x15 -> x30, local copies, waits for them, and re-layouts: 18.2 us -> 17.6 us
  transfers between devices with their start and end apart: 6 -> 6, of which waited for: 6 -> 5; matrix products, arithmetic and copies ran while one was open for 9% -> 12% of each run, Pallas kernels for 0% -> 0%
where the time goes in v1:
time: 362 us; the launch traced here: 361 us
  waiting for transfers between devices  252 us (70%)
  local copies, waits for them, and re-layouts  50.9 us (14%)
  starting transfers between devices  28 us (8%)
  between operations  13.7 us (4%)
  matrix products  10.3 us (3%)
  other arithmetic  5.99 us (2%)
    all_gather x1, waiting for transfers between devices, shards(): lax.all_gather(w_out, ('cfg', 'seq'), axis=0, tiled=True)  131 us
    all_gather x1, waiting for transfers between devices, shards(): lax.all_gather(jnp.concatenate([local_values, far_values[None]], 0), 'seq...  118 us
    all_to_all x1, starting transfers between devices, play_the_scenes(): lax.all_to_all(jnp.stack(lax.axis_size('seq') * [view]), 'seq', 0, 0)  18.4 us
    unnamed x30, local copies, waits for them, and re-layouts  17.6 us
    slice x2, local copies, waits for them, and re-layouts, shards(): group_values[0]  10 us
    ppermute x3, starting transfers between devices, from_partner(): lax.ppermute(x, axis, [(i, i ^ 1 << apart) for i in range(lax.axis_size(a...  9.55 us
    concatenate x4, local copies, waits for them, and re-layouts, shards(): jnp.concatenate([group_keys[1], pair_keys], 0)  7.36 us
  transfers between devices with their start and end apart: 6, of which 5 were waited for; matrix products, arithmetic and copies ran while one was open for 12% of the time, Pallas kernels for 0%

profile of v1, /device:TPU:1, one launch (start us, length us, event | category | flops | bytes accessed | tf_op | source)
XLA Modules:
  0.0 360.8 jit_solution(11261887712336749554)
XLA Ops:
  7.3 4.0 %collective-permute-start.1 = (bf16[2,2432]{1,0:T(2,128)(2,1)S(1)}, bf16[2,2432]{1,0:T(2,128)(2,1)S(1)}, u32[]{:S(2)}, u32[]{:S(2)}) collective-permute-start(bf16[2,2432]{1,0:T(2,128)(2,1)S(1)} %slice_bitcast_fusion.1), channel_id=1, source_target_pairs={{0,64},{64,0},{128,192},{192,128},{1,65},{65,1},{129,193},{193,129... | collective-permute-start | bytes 29192 | tf_op jit(solution)/shard_map/ppermute | solution.py:13
  14.5 3.4 collective-permute-start
  17.9 1.4 collective-permute-done
  20.1 2.2 stack.8
  22.3 18.4 %all-to-all-start = ((bf16[64,3,2,2432]{3,2,1,0:T(2,128)(2,1)}), bf16[64,3,2,2432]{3,2,1,0:T(2,128)(2,1)S(1)}, u32[]{:S(2)}, u32[]{:S(2)}) async-start(bf16[64,3,2,2432]{3,2,1,0:T(2,128)(2,1)} %stack.8), calls=%async_computation | async-start | bytes 3735552 | tf_op jit(solution)/shard_map/all_to_all | solution.py:64
  42.9 1.3 iota_compare_fusion.3
  44.3 1.2 fusion.67
  46.1 117.8 %all-gather.4.cloned.1.call-done = bf16[3,128,2432]{2,0,1:T(4,128)(2,1)} async-done(((bf16[3,2,2432]{2,0,1:T(4,128)(2,1)}), bf16[3,128,2432]{2,0,1:T(4,128)(2,1)}) %all-gather.4.cloned.1.call-update) | async-done | bytes 1867792 | tf_op jit(solution)/shard_map/all_gather | solution.py:69
  163.9 8.0 %fusion.74 = (bf16[1,128,2432]{2,0,1:T(2,128)(2,1)S(1)}, bf16[1,128,2432]{2,0,1:T(2,128)(2,1)}, bf16[1,128,2432]{2,0,1:T(2,128)(2,1)}) fusion(bf16[3,128,2432]{2,0,1:T(4,128)(2,1)} %all-gather.4.cloned.1.call-done), kind=kLoop, calls=%fused_computation.84 | loop fusion | bytes 3735552 | tf_op jit(solution)/shard_map/slice | solution.py:81
  171.9 3.6 copy.52
  175.4 3.6 copy.51
  179.0 2.0 copy.46
  181.1 2.1 fusion.75
  183.2 2.7 concatenate.29
  186.0 1.8 copy.49
  187.7 1.1 concatenate.28
  188.8 1.8 copy.48
  190.6 1.5 fusion.78
  193.0 1.1 reshape_squeeze.12
  194.0 0.8 fusion.79
  195.7 131.0 %all-gather.6.cloned.1.call-done = bf16[128,19,2432]{2,1,0:T(8,128)(2,1)} async-done(((bf16[1,19,2432]{2,1,0:T(8,128)(2,1)}), bf16[128,19,2432]{2,1,0:T(8,128)(2,1)}) %all-gather.6.cloned.1.call-update) | async-done | bytes 11829264 | tf_op jit(solution)/shard_map/all_gather | solution.py:93
  326.7 16.8 %reshape.90 = bf16[2432,2432,1]{1,0,2:T(8,128)(2,1)} reshape(bf16[128,19,2432]{2,1,0:T(8,128)(2,1)} %all-gather.6.cloned.1.call-done) | data formatting | bytes 23658496
  343.5 6.2 %fusion.80 = (f32[2,2]{1,0:T(2,128)S(1)}, f32[2,2,2432]{2,1,0:T(2,128)S(1)}) fusion(bf16[2432,2432,1]{1,0,2:T(8,128)(2,1)} %reshape.90, bf16[1,2,2432]{2,1,0:T(2,128)(2,1)S(1)} %stack_reshape.9, bf16[1,2,2432]{2,1,0:T(2,128)(2,1)S(1)} %stack_reshape.8, f32[2,2432]{1,0:T(2,128)S(1)} %fusion.43, bf16[1,1,2,2,2432]{4,3,2,1,0:T(2,128)(2,1)S(1)} %copy-done.7), kind=kOutput, calls=%fused_computation.90 | convolution fusion | flops 47394812 | bytes 11926544 | tf_op jit(solution)/shard_map/dot_general | solution.py:91
  350.3 2.2 collective-permute-start.2
  (69 shorter events, 11.1 us)
Async XLA Ops:
  6.5 343.4 %copy-start = (bf16[2432,64]{0,1:T(8,128)(2,1)S(1)}, bf16[2432,64]{0,1:T(8,128)(2,1)}, u32[]{:S(2)}) copy-start(bf16[2432,64]{0,1:T(8,128)(2,1)} %param.23) | copy-start | bytes 933892
  6.5 157.3 %all-gather.4.cloned.1.call-start = ((), (), s32[]{:S(2)}) async-start(), calls=%async_computation.1 | async-start | bytes 2529280 | tf_op jit(solution)/shard_map/all_gather | solution.py:69
  7.3 5.1 %collective-permute-start.1 = (bf16[2,2432]{1,0:T(2,128)(2,1)S(1)}, bf16[2,2432]{1,0:T(2,128)(2,1)S(1)}, u32[]{:S(2)}, u32[]{:S(2)}) collective-permute-start(bf16[2,2432]{1,0:T(2,128)(2,1)S(1)} %slice_bitcast_fusion.1), channel_id=1, source_target_pairs={{0,64},{64,0},{128,192},{192,128},{1,65},{65,1},{129,193},{193,129... | collective-permute-start | bytes 29192 | tf_op jit(solution)/shard_map/ppermute | solution.py:13
  13.1 313.6 %all-gather.6.cloned.1.call-start = ((), (), s32[]{:S(2)}) async-start(), calls=%async_computation.2 | async-start | bytes 15058944 | tf_op jit(solution)/shard_map/all_gather | solution.py:93
  14.5 4.7 %collective-permute-start = (bf16[2,2432]{1,0:T(2,128)(2,1)S(1)}, bf16[2,2432]{1,0:T(2,128)(2,1)S(1)}, u32[]{:S(2)}, u32[]{:S(2)}) collective-permute-start(bf16[2,2432]{1,0:T(2,128)(2,1)S(1)} %slice_bitcast_fusion.2), channel_id=1, source_target_pairs={{0,64},{64,0},{128,192},{192,128},{1,65},{65,1},{129,193},{193,129... | collective-permute-start | bytes 29192 | tf_op jit(solution)/shard_map/ppermute | solution.py:13
  22.3 18.5 %copy-start.8 = (bf16[1,1,2,2,2432]{4,3,2,1,0:T(2,128)(2,1)S(1)}, bf16[1,1,2,2,2432]{4,3,2,1,0:T(2,128)(2,1)}, u32[]{:S(2)}) copy-start(bf16[1,1,2,2,2432]{4,3,2,1,0:T(2,128)(2,1)} %param.13) | copy-start | bytes 58372
  22.3 18.6 %copy-start.9 = (s32[4,2]{0,1:T(2,128)S(1)}, s32[4,2]{0,1:T(2,128)}, u32[]{:S(2)}) copy-start(s32[4,2]{0,1:T(2,128)} %param.19) | copy-start | bytes 100
  22.3 19.3 %copy-start.11 = (s32[4,2]{0,1:T(2,128)S(1)}, s32[4,2]{0,1:T(2,128)}, u32[]{:S(2)}) copy-start(s32[4,2]{0,1:T(2,128)} %param.18) | copy-start | bytes 100
  22.3 23.2 %copy-start.6 = (f32[1,6,2432]{2,0,1:T(1,128)S(1)}, f32[1,6,2432]{2,0,1:T(1,128)}, u32[]{:S(2)}) copy-start(f32[1,6,2432]{2,0,1:T(1,128)} %param.21) | copy-start | bytes 175108
  22.3 23.5 %copy-start.5 = (f32[1,6,2,2432]{3,2,1,0:T(2,128)S(1)}, f32[1,6,2,2432]{3,2,1,0:T(2,128)}, u32[]{:S(2)}) copy-start(f32[1,6,2,2432]{3,2,1,0:T(2,128)} %param.22) | copy-start | bytes 350212
  22.3 158.8 %all-to-all-start = ((bf16[64,3,2,2432]{3,2,1,0:T(2,128)(2,1)}), bf16[64,3,2,2432]{3,2,1,0:T(2,128)(2,1)S(1)}, u32[]{:S(2)}, u32[]{:S(2)}) async-start(bf16[64,3,2,2432]{3,2,1,0:T(2,128)(2,1)} %stack.8), calls=%async_computation | async-start | bytes 3735552 | tf_op jit(solution)/shard_map/all_to_all | solution.py:64
  188.8 1.8 copy-start.4
  190.6 1.7 copy-start.2
  190.6 1.7 copy-start.3
  194.0 1.1 copy-start.1
  195.7 147.7 %copy-start.7 = (bf16[1,1,2,2,2432]{4,3,2,1,0:T(2,128)(2,1)S(1)}, bf16[1,1,2,2,2432]{4,3,2,1,0:T(2,128)(2,1)}, u32[]{:S(2)}) copy-start(bf16[1,1,2,2,2432]{4,3,2,1,0:T(2,128)(2,1)} %param.16) | copy-start | bytes 58372
  343.5 9.0 %copy-start.12 = (f32[6]{0:T(128)S(1)}, f32[6]{0:T(128)}, u32[]{:S(2)}) copy-start(f32[6]{0:T(128)} %param.25) | copy-start | bytes 76
  343.5 9.0 %copy-start.13 = (f32[6]{0:T(128)S(1)}, f32[6]{0:T(128)}, u32[]{:S(2)}) copy-start(f32[6]{0:T(128)} %param.24) | copy-start | bytes 76
  343.5 9.9 %copy-start.10 = (f32[1,2,2,32]{3,2,1,0:T(2,128)S(1)}, f32[1,2,2,32]{3,2,1,0:T(2,128)}, u32[]{:S(2)}) copy-start(f32[1,2,2,32]{3,2,1,0:T(2,128)} %param.17) | copy-start | bytes 1540
  350.3 3.1 collective-permute-start.2
Sparse Core Ops, SparseCore 0:
  13.2 150.6 all-gather.3
  166.9 159.7 all-gather.5
